TPU v7x, 512 devices: a whole 4x8x8 slice. The times are simulated.
512 devices in a mesh: row: 8 (over x, y_lo), col: 8 (over y_hi, core), smp: 8 (over z).
Axes of the slice: x: 4, y: 8 (y_hi: 4, y_lo: 2; y = y_hi * 2 + y_lo), z: 8, core: 2. Of those that a mesh axis runs over, the one named last changes fastest.
Arguments:
- single: bfloat16 [1024, 768], P('row'), may hold values from -0.59765625 to 0.59765625
- pair_features: bfloat16 [1024, 1024, 128], P('row', ('col', 'smp')), may hold values from -6 to 6
- coords: float32 [3, 8192], replicated, may hold values from -6 to 6
- token_centre_atom: int32 [1024], P('row'), may hold values from 0 to 8191
- chain_label: int32 [1024], P('row'), may hold values from 0 to 7, never falling along the last dimension, each value on 1 to 256 neighbouring positions
- padding_key_mask: int32 [1024], P('row'), may hold values 0 or 1
- angles: float32 [8, 3], P('smp'), may hold values from -3.140625 to 3.140625
- sample_noise_level: float32 [8], P('smp'), may hold values from 0.05 to 10
- centre_noise: float32 [8, 3, 1024], P('smp', None, 'row'), may hold values from -6 to 6
- embedding_weight: float32 [4, 768], replicated, may hold values from -1.5 to 1.5
- pair_bias_weight: bfloat16 [128, 4, 16], replicated, may hold values from -1 to 1
- same_chain_offset: float32 [4, 16], replicated, may hold values from -300 to 300
- query_key_value_gate_weight: bfloat16 [4, 4, 768, 768], P(None, None, 'col'), may hold values from -0.21875 to 0.21875
- attention_output_weight: bfloat16 [4, 768, 768], P(None, 'col'), may hold values from -1.25 to 1.25
- position_update_weight: bfloat16 [3, 768], replicated, may hold values from -0.21875 to 0.21875
Outputs:
- tokens_out: bfloat16 [8, 1024, 768], P('smp', 'row')
- denoised: float32 [8, 3, 1024], P('smp', None, 'row')
All inputs are finite; a program needn't handle non-finite values. No bound on the sum of `padding_key_mask` on one device may be relied on, other than what follows from the above.
Results may differ from a plain program's by a relative error of at most 0.024.
Values may be sent and summed in bfloat16 or wider, within the bound.
No kernel may reach another device: no remote copies, remote signals or barrier semaphores. Data moves between devices by JAX's collectives and lax.ppermute only.
A program may use at most 64 MiB of HBM per device.

v0:
```python
import jax
import jax.numpy as jnp
from jax import lax
from jax.sharding import PartitionSpec as P

EPSILON = 1e-05
MASKED = -1000000000.0
LOWEST = -1e30


def layer_norm(inputs):
    average = jnp.mean(inputs, axis=-1, keepdims=True)
    centred = inputs - average
    spread = jnp.mean(centred * centred, axis=-1, keepdims=True)
    return centred * lax.rsqrt(spread + EPSILON)


def rotation_rows(angles):
    cos_a = jnp.cos(angles[:, 0])
    sin_a = jnp.sin(angles[:, 0])
    cos_b = jnp.cos(angles[:, 1])
    sin_b = jnp.sin(angles[:, 1])
    cos_c = jnp.cos(angles[:, 2])
    sin_c = jnp.sin(angles[:, 2])
    first = jnp.stack(
        [
            cos_a * cos_b,
            cos_a * sin_b * sin_c - sin_a * cos_c,
            cos_a * sin_b * cos_c + sin_a * sin_c,
        ],
        axis=-1,
    )
    second = jnp.stack(
        [
            sin_a * cos_b,
            sin_a * sin_b * sin_c + cos_a * cos_c,
            sin_a * sin_b * cos_c - cos_a * sin_c,
        ],
        axis=-1,
    )
    third = jnp.stack([-sin_b, cos_b * sin_c, cos_b * cos_c], axis=-1)
    return jnp.stack([first, second, third], axis=1)


def noisy_centres(coords, token_centre_atom, angles, sample_noise_level, centre_noise):
    centre = jnp.take(coords, token_centre_atom, axis=1)
    rotation = rotation_rows(angles)
    turned = rotation[:, :, 0, None] * centre[0][None, None, :]
    turned = turned + rotation[:, :, 1, None] * centre[1][None, None, :]
    turned = turned + rotation[:, :, 2, None] * centre[2][None, None, :]
    return turned + sample_noise_level[:, None, None] * centre_noise


def embed_tokens(single, noisy, sample_noise_level, embedding_weight):
    scaled = noisy / jnp.sqrt(sample_noise_level * sample_noise_level + 1.0)[:, None, None]
    log_level = 0.25 * jnp.log(sample_noise_level)
    hidden_activity = single.astype(jnp.float32)[None] + scaled[:, 0, :, None] * embedding_weight[0]
    hidden_activity = hidden_activity + scaled[:, 1, :, None] * embedding_weight[1]
    hidden_activity = hidden_activity + scaled[:, 2, :, None] * embedding_weight[2]
    hidden_activity = hidden_activity + log_level[:, None, None] * embedding_weight[3]
    return hidden_activity.astype(jnp.bfloat16)


def relay_bias(local_bias):
    blocks, total_heads, row_count, keys_dev = local_bias.shape
    col_count = lax.axis_size("col")
    copies = lax.axis_size("smp")
    group_members = total_heads // col_count
    spread = jnp.broadcast_to(
        local_bias.reshape(blocks, col_count, 1, group_members, row_count, 1, keys_dev),
        (blocks, col_count, copies, group_members, row_count, 1, keys_dev),
    )
    spread = spread.reshape(blocks, col_count * copies * group_members, row_count, 1, keys_dev)
    relayed = lax.all_to_all(spread, ("col", "smp"), split_axis=1, concat_axis=3, tiled=True)
    return relayed.reshape(blocks, group_members, row_count, -1)


def build_absorber(
    query_vectors,
    per_block_bias,
    chain_offset,
    query_chain_labels,
    gathered_chain_ids,
    gathered_key_mask,
    input_scaling,
):
    samples, row_count, group_members, head_size = query_vectors.shape

    def absorb(running, kv_piece, key_start):
        key_count = kv_piece.shape[0]
        key_rows = kv_piece[:, :, 0].reshape(key_count, samples, group_members, head_size)
        value_rows = kv_piece[:, :, 1].reshape(key_count, samples, group_members, head_size)
        attention_logits = (
            jnp.einsum(
                "sqhd,kshd->shqk", query_vectors, key_rows, preferred_element_type=jnp.float32
            )
            * input_scaling
        )
        bias_section = per_block_bias.astype(jnp.float32)
        chain_match = (query_chain_labels[:, None] == gathered_chain_ids[None, :]).astype(
            jnp.float32
        )
        attention_logits = (
            attention_logits
            + bias_section[None]
            + chain_offset[None, :, None, None] * chain_match[None, None]
        )
        attention_logits = jnp.where(
            gathered_key_mask[None, None, None, :] > 0, attention_logits, MASKED
        )
        old_max, old_sum, old_acc = running
        new_max = jnp.maximum(old_max, jnp.max(attention_logits, axis=-1))
        unscaled = jnp.exp(attention_logits - new_max[..., None])
        new_sum = jnp.sum(unscaled, axis=-1)
        new_acc = jnp.einsum(
            "shqk,kshd->shqd",
            unscaled.astype(jnp.bfloat16),
            value_rows,
            preferred_element_type=jnp.float32,
        )
        return (new_max, new_sum, new_acc)

    return absorb


def body(
    single,
    pair_features,
    coords,
    token_centre_atom,
    chain_label,
    padding_key_mask,
    angles,
    sample_noise_level,
    centre_noise,
    embedding_weight,
    pair_bias_weight,
    same_chain_offset,
    query_key_value_gate_weight,
    attention_output_weight,
    position_update_weight,
):
    noisy = noisy_centres(coords, token_centre_atom, angles, sample_noise_level, centre_noise)
    hidden_activity = embed_tokens(single, noisy, sample_noise_level, embedding_weight)
    pair_normed = layer_norm(pair_features.astype(jnp.float32)).astype(jnp.bfloat16)
    local_bias = jnp.einsum(
        "ikc,cbh->bhik", pair_normed, pair_bias_weight, preferred_element_type=jnp.float32
    ).astype(jnp.bfloat16)
    gathered_pair_bias = relay_bias(local_bias)
    gathered_chain_ids, gathered_key_mask = (
        lax.all_gather(chain_label, "row", axis=0, tiled=True),
        lax.all_gather(padding_key_mask, "row", axis=0, tiled=True),
    )
    samples, row_count, model_width = hidden_activity.shape
    group_members = gathered_pair_bias.shape[1]
    head_size = query_key_value_gate_weight.shape[2] // group_members
    group_offset = lax.axis_index("col") * group_members
    input_scaling = head_size ** (-0.5)
    for block_index in range(query_key_value_gate_weight.shape[0]):
        normed = layer_norm(hidden_activity.astype(jnp.float32)).astype(jnp.bfloat16)
        front = jnp.einsum(
            "snd,fed->fsne",
            normed,
            query_key_value_gate_weight[block_index, 0:2],
            preferred_element_type=jnp.float32,
        )
        key_value = jnp.einsum(
            "snd,fed->nsfe",
            normed,
            query_key_value_gate_weight[block_index, 2:4],
            preferred_element_type=jnp.float32,
        ).astype(jnp.bfloat16)
        query_vectors = (
            front[0].astype(jnp.bfloat16).reshape(samples, row_count, group_members, head_size)
        )
        chain_offset = lax.dynamic_slice_in_dim(
            same_chain_offset[block_index], group_offset, group_members, 0
        )
        absorb = build_absorber(
            query_vectors,
            gathered_pair_bias[block_index],
            chain_offset,
            chain_label,
            gathered_chain_ids,
            gathered_key_mask,
            input_scaling,
        )
        start_state = (
            jnp.full((samples, group_members, row_count), LOWEST, jnp.float32),
            jnp.zeros((samples, group_members, row_count), jnp.float32),
            jnp.zeros((samples, group_members, row_count, head_size), jnp.float32),
        )
        final_max, final_sum, final_acc = absorb(
            start_state, lax.all_gather(key_value, "row", axis=0, tiled=True), jnp.int32(0)
        )
        attended = final_acc / final_sum[..., None]
        attended = jnp.transpose(attended, (0, 2, 1, 3)).reshape(
            samples, row_count, group_members * head_size
        )
        gated_output = (jax.nn.sigmoid(front[1]) * attended).astype(jnp.bfloat16)
        partial_out = jnp.einsum(
            "kxp,pj->kxj",
            gated_output,
            attention_output_weight[block_index],
            preferred_element_type=jnp.float32,
        )
        summed = lax.psum(partial_out.astype(jnp.bfloat16), "col").astype(jnp.float32)
        hidden_activity = (hidden_activity.astype(jnp.float32) + summed).astype(jnp.bfloat16)
    final_normed = layer_norm(hidden_activity.astype(jnp.float32)).astype(jnp.bfloat16)
    update = jnp.einsum(
        "snd,cd->scn", final_normed, position_update_weight, preferred_element_type=jnp.float32
    )
    spread_sq = 1.0 + sample_noise_level * sample_noise_level
    denoised = (
        noisy / spread_sq[:, None, None]
        + (sample_noise_level / jnp.sqrt(spread_sq))[:, None, None] * update
    )
    return (hidden_activity, denoised)


def solution(mesh):
    return jax.shard_map(
        body,
        mesh=mesh,
        in_specs=(
            P("row", None),
            P("row", ("col", "smp"), None),
            P(),
            P("row"),
            P("row"),
            P("row"),
            P("smp", None),
            P("smp"),
            P("smp", None, "row"),
            P(),
            P(),
            P(),
            P(None, None, "col", None),
            P(None, "col", None),
            P(),
        ),
        out_specs=(P("smp", "row", None), P("smp", None, "row")),
        check_vma=False,
    )
```

profile of v0, /device:TPU:17, one launch (start us, length us, event | category | flops | bytes accessed | tf_op | source)
XLA Modules:
  0.0 548.1 jit_solution(17188569693350493762)
XLA Ops:
  7.2 1.4 convert_reduce_fusion
  8.6 1.7 fusion.36
  10.3 1.6 fusion.50
  12.0 0.3 convolution_convert_fusion
  12.4 1.9 broadcast_in_dim.47
  14.3 16.9 %all-to-all-start = ((bf16[4,128,128,1,16]{2,4,3,0,1:T(8,128)(2,1)}), bf16[4,128,128,1,16]{2,4,3,0,1:T(8,128)(2,1)S(1)}, u32[]{:S(2)}, u32[]{:S(2)}) async-start(bf16[4,128,128,1,16]{2,4,3,0,1:T(8,128)(2,1)} %bitcast.262), calls=%async_computation | async-start | bytes 4194304 | tf_op jit(solution)/shard_map/all_to_all | solution.py:74
  31.3 0.6 fusion.149
  36.9 2.6 copy.35
  39.5 2.8 gather_fusion
  42.9 0.2 slice_reduce_fusion.2
  43.2 0.3 convert_reduce_fusion.4
  43.5 0.2 fusion.72
  43.7 1.3 convolution_bitcast_fusion.3
  45.0 41.1 %all-gather.1 = s32[8,1,128]{2,1,0:T(1,128)S(1)} all-gather(s32[1,1,128]{2,1,0:T(1,128)S(1)} %bitcast.290), channel_id=1, replica_groups=mesh['row'=8,'col'=8,'smp'=8] {'row'}, dimensions={0}, use_global_device_ids=true | all-gather | bytes 4608 | tf_op jit(solution)/shard_map/all_gather | solution.py:151
  86.1 11.5 %all-gather = s32[8,1,128]{2,1,0:T(1,128)S(1)} all-gather(s32[1,1,128]{2,1,0:T(1,128)S(1)} %bitcast.291), channel_id=1, replica_groups=mesh['row'=8,'col'=8,'smp'=8] {'row'}, dimensions={0}, use_global_device_ids=true | all-gather | bytes 4608 | tf_op jit(solution)/shard_map/all_gather | solution.py:152
  97.7 1.3 fusion.22
  99.0 21.4 %all_gather.19 = bf16[1024,1,2,96]{0,3,2,1:T(8,128)(2,1)S(1)} all-gather(bf16[128,1,2,96]{0,3,2,1:T(8,128)(2,1)S(1)} %fusion.22), channel_id=1, replica_groups=mesh['row'=8,'col'=8,'smp'=8] {'row'}, dimensions={0}, use_global_device_ids=true | all-gather | bytes 442368 | tf_op jit(solution)/shard_map/all_gather | solution.py:194
  120.6 0.4 copy.40
  121.0 1.9 slice_convert_fusion
  122.9 1.3 copy.42
  124.2 1.7 fusion.150
  125.9 0.3 fusion.38
  126.2 0.4 fusion.33
  126.6 1.8 fusion.14
  128.5 1.3 copy.43
  129.8 1.4 copy.44
  131.2 85.6 %all-reduce.5.cloned.1.call-done = bf16[1,128,768]{2,1,0:T(8,128)(2,1)} async-done(((bf16[1,128,768]{2,1,0:T(8,128)(2,1)}), bf16[1,128,768]{2,1,0:T(8,128)(2,1)}) %all-reduce.5.cloned.1.call-update) | async-done | bytes 196624 | tf_op jit(solution)/shard_map/psum | solution.py:207
  216.9 1.1 convert_reduce_fusion.3
  217.9 0.2 fusion.70
  218.1 1.3 fusion.23
  219.4 1.3 convolution_bitcast_fusion.2
  220.7 21.4 %all_gather.21 = bf16[1024,1,2,96]{0,3,2,1:T(8,128)(2,1)S(1)} all-gather(bf16[128,1,2,96]{0,3,2,1:T(8,128)(2,1)S(1)} %fusion.23), channel_id=1, replica_groups=mesh['row'=8,'col'=8,'smp'=8] {'row'}, dimensions={0}, use_global_device_ids=true | all-gather | bytes 442368 | tf_op jit(solution)/shard_map/all_gather | solution.py:194
  242.2 0.5 fusion.151
  242.7 0.3 fusion.40
  243.0 0.4 fusion.32
  243.4 1.8 fusion.15
  245.4 1.3 copy.45
  246.7 1.3 copy.46
  248.0 77.0 %all-reduce.7.cloned.1.call-done = bf16[1,128,768]{2,1,0:T(8,128)(2,1)} async-done(((bf16[1,128,768]{2,1,0:T(8,128)(2,1)}), bf16[1,128,768]{2,1,0:T(8,128)(2,1)}) %all-reduce.7.cloned.1.call-update) | async-done | bytes 196624 | tf_op jit(solution)/shard_map/psum | solution.py:207
  325.1 1.1 convert_reduce_fusion.2
  326.1 0.2 fusion.68
  326.3 1.3 fusion.24
  327.6 1.3 convolution_bitcast_fusion.1
  328.9 21.5 %all_gather.22 = bf16[1024,1,2,96]{0,3,2,1:T(8,128)(2,1)S(1)} all-gather(bf16[128,1,2,96]{0,3,2,1:T(8,128)(2,1)S(1)} %fusion.24), channel_id=1, replica_groups=mesh['row'=8,'col'=8,'smp'=8] {'row'}, dimensions={0}, use_global_device_ids=true | all-gather | bytes 442368 | tf_op jit(solution)/shard_map/all_gather | solution.py:194
  350.5 0.5 fusion.152
  351.0 0.3 fusion.42
  351.3 0.4 fusion.31
  351.7 0.9 fusion.16
  352.6 0.2 all-reduce.11.cloned.1.call-start
  352.9 0.3 copy.48
  353.3 79.0 %all-reduce.9.cloned.1.call-done = bf16[1,128,768]{2,1,0:T(8,128)(2,1)} async-done(((bf16[1,128,768]{2,1,0:T(8,128)(2,1)}), bf16[1,128,768]{2,1,0:T(8,128)(2,1)}) %all-reduce.9.cloned.1.call-update) | async-done | bytes 196624 | tf_op jit(solution)/shard_map/psum | solution.py:207
  432.3 1.1 convert_reduce_fusion.1
  433.3 0.2 fusion.66
  433.5 1.3 fusion.25
  434.8 1.3 convolution_bitcast_fusion
  436.1 21.4 %all_gather.23 = bf16[1024,1,2,96]{0,3,2,1:T(8,128)(2,1)S(1)} all-gather(bf16[128,1,2,96]{0,3,2,1:T(8,128)(2,1)S(1)} %fusion.25), channel_id=1, replica_groups=mesh['row'=8,'col'=8,'smp'=8] {'row'}, dimensions={0}, use_global_device_ids=true | all-gather | bytes 442368 | tf_op jit(solution)/shard_map/all_gather | solution.py:194
  457.6 0.5 fusion.153
  458.1 0.3 fusion.44
  458.4 0.4 fusion.30
  458.8 0.9 fusion.17
  459.8 79.7 %all-reduce.11.cloned.1.call-done = bf16[1,128,768]{2,1,0:T(8,128)(2,1)} async-done(((bf16[1,128,768]{2,1,0:T(8,128)(2,1)}), bf16[1,128,768]{2,1,0:T(8,128)(2,1)}) %all-reduce.11.cloned.1.call-update) | async-done | bytes 196624 | tf_op jit(solution)/shard_map/psum | solution.py:207
  539.4 1.1 convert_reduce_fusion.5
  540.7 0.2 fusion.35
  540.9 0.6 copy.49
  (86 shorter events, 2.0 us)
Async XLA Ops:
  7.2 4.8 copy-start
  14.3 17.0 %copy-start.8 = (f32[1,3]{1,0:T(1,128)S(1)}, f32[1,3]{1,0:T(1,128)}, u32[]{:S(2)}) copy-start(f32[1,3]{1,0:T(1,128)} %param.21) | copy-start | bytes 40
  14.3 17.6 %copy-start.14 = (s32[128]{0:T(128)S(1)}, s32[128]{0:T(128)}, u32[]{:S(2)}) copy-start(s32[128]{0:T(128)} %param.18) | copy-start | bytes 1540
  14.3 22.5 %copy-start.6 = (f32[3,8192]{1,0:T(4,128)S(1)}, f32[3,8192]{1,0:T(4,128)}, u32[]{:S(2)}) copy-start(f32[3,8192]{1,0:T(4,128)} %param.17) | copy-start | bytes 294916
  14.3 106.3 %all-to-all-start = ((bf16[4,128,128,1,16]{2,4,3,0,1:T(8,128)(2,1)}), bf16[4,128,128,1,16]{2,4,3,0,1:T(8,128)(2,1)S(1)}, u32[]{:S(2)}, u32[]{:S(2)}) async-start(bf16[4,128,128,1,16]{2,4,3,0,1:T(8,128)(2,1)} %bitcast.262), calls=%async_computation | async-start | bytes 4194304 | tf_op jit(solution)/shard_map/all_to_all | solution.py:74
  31.3 11.5 %copy-start.7 = (f32[4,768]{1,0:T(4,128)S(1)}, f32[4,768]{1,0:T(4,128)}, u32[]{:S(2)}) copy-start(f32[4,768]{1,0:T(4,128)} %param.24) | copy-start | bytes 36868
  31.3 185.6 %all-reduce.5.cloned.1.call-start = ((), (), s32[]{:S(2)}) async-start(), calls=%async_computation.1 | async-start | bytes 393216 | tf_op jit(solution)/shard_map/psum | solution.py:207
  36.8 6.2 %copy-start.11 = (f32[1,3,128]{2,0,1:T(1,128)S(1)}, f32[1,3,128]{2,0,1:T(1,128)}, u32[]{:S(2)}) copy-start(f32[1,3,128]{2,0,1:T(1,128)} %param.23) | copy-start | bytes 4612
  36.9 6.3 %copy-start.5 = (bf16[128,768]{1,0:T(8,128)(2,1)S(1)}, bf16[128,768]{1,0:T(8,128)(2,1)}, u32[]{:S(2)}) copy-start(bf16[128,768]{1,0:T(8,128)(2,1)} %param.15) | copy-start | bytes 589828
  36.9 8.1 %copy-start.9 = (s32[128]{0:T(128)S(1)}, s32[128]{0:T(128)}, u32[]{:S(2)}) copy-start(s32[128]{0:T(128)} %param.19) | copy-start | bytes 1540
  36.9 49.2 %copy-start.12 = (s32[128]{0:T(128)S(1)}, s32[128]{0:T(128)}, u32[]{:S(2)}) copy-start(s32[128]{0:T(128)} %param.20) | copy-start | bytes 1540
  36.9 60.7 %copy-start.10 = (f32[4,16]{1,0:T(4,128)S(1)}, f32[4,16]{1,0:T(4,128)}, u32[]{:S(2)}) copy-start(f32[4,16]{1,0:T(4,128)} %param.26) | copy-start | bytes 772
  128.5 196.6 %all-reduce.7.cloned.1.call-start = ((), (), s32[]{:S(2)}) async-start(), calls=%async_computation.2 | async-start | bytes 393216 | tf_op jit(solution)/shard_map/psum | solution.py:207
  131.2 111.0 %copy-start.1 = (f32[2,128,1024]{2,1,0:T(8,128)S(1)}, f32[2,128,1024]{2,1,0:T(8,128)}, u32[]{:S(2)}) copy-start(f32[2,128,1024]{2,1,0:T(8,128)} %copy.44) | copy-start | bytes 3145732
  245.3 187.0 %all-reduce.9.cloned.1.call-start = ((), (), s32[]{:S(2)}) async-start(), calls=%async_computation.3 | async-start | bytes 393216 | tf_op jit(solution)/shard_map/psum | solution.py:207
  248.0 102.4 %copy-start.2 = (f32[2,128,1024]{2,1,0:T(8,128)S(1)}, f32[2,128,1024]{2,1,0:T(8,128)}, u32[]{:S(2)}) copy-start(f32[2,128,1024]{2,1,0:T(8,128)} %copy.46) | copy-start | bytes 3145732
  350.4 1.2 copy-start.4
  352.6 186.8 %all-reduce.11.cloned.1.call-start = ((), (), s32[]{:S(2)}) async-start(), calls=%async_computation.4 | async-start | bytes 393216 | tf_op jit(solution)/shard_map/psum | solution.py:207
  458.1 82.6 %copy-start.13 = (bf16[3,768]{1,0:T(4,128)(2,1)S(1)}, bf16[3,768]{1,0:T(4,128)(2,1)}, u32[]{:S(2)}) copy-start(bf16[3,768]{1,0:T(4,128)(2,1)} %param.29) | copy-start | bytes 13828
  540.5 1.1 copy-start.3
Sparse Core Ops, SparseCore 0:
  128.6 88.2 all-reduce.4
  245.4 79.6 all-reduce.6
  352.7 79.4 all-reduce.8
  459.8 79.5 all-reduce.10
where the time goes:
time: 549 us; the launch traced here: 548 us
  waiting for transfers between devices  321 us (58%)
  blocking collectives  138 us (25%)
  matrix products  20.9 us (4%)
  between operations  19.3 us (4%)
  starting transfers between devices  17.3 us (3%)
  local copies, waits for them, and re-layouts  16.9 us (3%)
  other arithmetic  14 us (3%)
    psum x4, waiting for transfers between devices, body(): lax.psum(partial_out.astype(jnp.bfloat16), 'col').astype(jnp.float32)  321 us
    all_gather x4, blocking collectives, body(): lax.all_gather(key_value, 'row', axis=0, tiled=True)  85.7 us
    all_gather x1, blocking collectives, body(): lax.all_gather(chain_label, 'row', axis=0, tiled=True)  41.1 us
    all_to_all x1, starting transfers between devices, relay_bias(): lax.all_to_all(spread, ('col', 'smp'), split_axis=1, concat_axis=3, tiled...  16.9 us
    all_gather x1, blocking collectives, body(): lax.all_gather(padding_key_mask, 'row', axis=0, tiled=True)  11.5 us
  transfers between devices with their start and end apart: 5, of which 4 were waited for; matrix products, arithmetic and copies ran while one was open for 3% of the time, Pallas kernels for 0%

commit v1 on v0

--- a/solution.py
+++ b/solution.py
@@ -148,7 +148,9 @@
     ).astype(jnp.bfloat16)
     gathered_pair_bias = relay_bias(local_bias)
     gathered_chain_ids, gathered_key_mask = (
-        lax.all_gather(chain_label, "row", axis=0, tiled=True),
+        jnp.concatenate(
+            lax.all_to_all(jnp.stack([chain_label] * lax.axis_size("row")), "row", 0, 0), axis=0
+        ),
         lax.all_gather(padding_key_mask, "row", axis=0, tiled=True),
     )
     samples, row_count, model_width = hidden_activity.shape

time: 549 us -> 542 us (0.987)
  blocking collectives: 138 us -> 128 us
    all_gather x1 -> x0, blocking collectives: 41.1 us -> none  [body(): lax.all_gather(chain_label, 'row', axis=0, tiled=True)]
    all_gather x1, blocking collectives: 11.5 us -> 42.1 us  [body(): lax.all_gather(padding_key_mask, 'row', axis=0, tiled=True)]
  transfers between devices with their start and end apart: 5 -> 6, of which waited for: 4 -> 4; matrix products, arithmetic and copies ran while one was open for 3% -> 4% of each run, Pallas kernels for 0% -> 0%
where the time goes in v1:
time: 542 us; the launch traced here: 541 us
  waiting for transfers between devices  318 us (59%)
  blocking collectives  128 us (24%)
  starting transfers between devices  21.7 us (4%)
  matrix products  20.9 us (4%)
  between operations  19.4 us (4%)
  local copies, waits for them, and re-layouts  18.3 us (3%)
  other arithmetic  14.6 us (3%)
    psum x4, waiting for transfers between devices, body(): lax.psum(partial_out.astype(jnp.bfloat16), 'col').astype(jnp.float32)  318 us
    all_gather x4, blocking collectives, body(): lax.all_gather(key_value, 'row', axis=0, tiled=True)  86 us
    all_gather x1, blocking collectives, body(): lax.all_gather(padding_key_mask, 'row', axis=0, tiled=True)  42.1 us
    all_to_all x1, starting transfers between devices, relay_bias(): lax.all_to_all(spread, ('col', 'smp'), split_axis=1, concat_axis=3, tiled...  16.3 us
  transfers between devices with their start and end apart: 6, of which 4 were waited for; matrix products, arithmetic and copies ran while one was open for 4% of the time, Pallas kernels for 0%

profile of v1, /device:TPU:17, one launch (start us, length us, event | category | flops | bytes accessed | tf_op | source)
XLA Modules:
  0.0 541.1 jit_solution(865129464383877281)
XLA Ops:
  7.2 1.3 stack.75
  8.5 5.0 all-to-all-start.1
  13.5 0.7 compare_select_fusion
  14.1 1.4 convert_reduce_fusion
  15.5 1.7 fusion.36
  17.3 1.6 fusion.50
  18.9 0.3 convolution_convert_fusion
  19.2 0.7 fusion.149
  20.1 1.9 broadcast_in_dim.47
  21.9 16.3 %all-to-all-start = ((bf16[4,128,128,1,16]{2,4,3,0,1:T(8,128)(2,1)}), bf16[4,128,128,1,16]{2,4,3,0,1:T(8,128)(2,1)S(1)}, u32[]{:S(2)}, u32[]{:S(2)}) async-start(bf16[4,128,128,1,16]{2,4,3,0,1:T(8,128)(2,1)} %bitcast.261), calls=%async_computation | async-start | bytes 4194304 | tf_op jit(solution)/shard_map/all_to_all | solution.py:74
  43.4 2.6 copy.35
  46.0 2.8 gather_fusion
  49.7 0.3 convert_reduce_fusion.4
  50.0 0.2 fusion.72
  50.2 1.3 convolution_bitcast_fusion.3
  51.5 42.1 %all-gather = s32[8,1,128]{2,1,0:T(1,128)S(1)} all-gather(s32[1,1,128]{2,1,0:T(1,128)S(1)} %bitcast.289), channel_id=1, replica_groups=mesh['row'=8,'col'=8,'smp'=8] {'row'}, dimensions={0}, use_global_device_ids=true | all-gather | bytes 4608 | tf_op jit(solution)/shard_map/all_gather | solution.py:154
  93.6 1.3 fusion.22
  94.9 21.6 %all_gather.16 = bf16[1024,1,2,96]{0,3,2,1:T(8,128)(2,1)S(1)} all-gather(bf16[128,1,2,96]{0,3,2,1:T(8,128)(2,1)S(1)} %fusion.22), channel_id=1, replica_groups=mesh['row'=8,'col'=8,'smp'=8] {'row'}, dimensions={0}, use_global_device_ids=true | all-gather | bytes 442368 | tf_op jit(solution)/shard_map/all_gather | solution.py:196
  116.7 0.4 copy.40
  117.1 1.9 slice_convert_fusion
  119.0 1.3 copy.42
  120.3 1.7 fusion.150
  122.1 0.3 fusion.38
  122.4 0.4 fusion.33
  122.7 1.8 fusion.14
  124.7 1.3 copy.43
  126.0 1.4 copy.44
  127.3 82.6 %all-reduce.5.cloned.1.call-done = bf16[1,128,768]{2,1,0:T(8,128)(2,1)} async-done(((bf16[1,128,768]{2,1,0:T(8,128)(2,1)}), bf16[1,128,768]{2,1,0:T(8,128)(2,1)}) %all-reduce.5.cloned.1.call-update) | async-done | bytes 196624 | tf_op jit(solution)/shard_map/psum | solution.py:209
  210.0 1.1 convert_reduce_fusion.3
  211.0 0.2 fusion.70
  211.2 1.3 fusion.23
  212.5 1.3 convolution_bitcast_fusion.2
  213.8 21.5 %all_gather.17 = bf16[1024,1,2,96]{0,3,2,1:T(8,128)(2,1)S(1)} all-gather(bf16[128,1,2,96]{0,3,2,1:T(8,128)(2,1)S(1)} %fusion.23), channel_id=1, replica_groups=mesh['row'=8,'col'=8,'smp'=8] {'row'}, dimensions={0}, use_global_device_ids=true | all-gather | bytes 442368 | tf_op jit(solution)/shard_map/all_gather | solution.py:196
  235.3 0.5 fusion.151
  235.8 0.3 fusion.40
  236.1 0.4 fusion.32
  236.5 1.8 fusion.15
  238.5 1.3 copy.45
  239.8 1.3 copy.46
  241.2 76.9 %all-reduce.7.cloned.1.call-done = bf16[1,128,768]{2,1,0:T(8,128)(2,1)} async-done(((bf16[1,128,768]{2,1,0:T(8,128)(2,1)}), bf16[1,128,768]{2,1,0:T(8,128)(2,1)}) %all-reduce.7.cloned.1.call-update) | async-done | bytes 196624 | tf_op jit(solution)/shard_map/psum | solution.py:209
  318.1 1.1 convert_reduce_fusion.2
  319.1 0.2 fusion.68
  319.3 1.3 fusion.24
  320.6 1.3 convolution_bitcast_fusion.1
  322.0 21.5 %all_gather.18 = bf16[1024,1,2,96]{0,3,2,1:T(8,128)(2,1)S(1)} all-gather(bf16[128,1,2,96]{0,3,2,1:T(8,128)(2,1)S(1)} %fusion.24), channel_id=1, replica_groups=mesh['row'=8,'col'=8,'smp'=8] {'row'}, dimensions={0}, use_global_device_ids=true | all-gather | bytes 442368 | tf_op jit(solution)/shard_map/all_gather | solution.py:196
  343.5 0.5 fusion.152
  344.0 0.3 fusion.42
  344.3 0.4 fusion.31
  344.7 0.9 fusion.16
  345.7 0.2 all-reduce.11.cloned.1.call-start
  346.0 0.3 copy.48
  346.3 78.9 %all-reduce.9.cloned.1.call-done = bf16[1,128,768]{2,1,0:T(8,128)(2,1)} async-done(((bf16[1,128,768]{2,1,0:T(8,128)(2,1)}), bf16[1,128,768]{2,1,0:T(8,128)(2,1)}) %all-reduce.9.cloned.1.call-update) | async-done | bytes 196624 | tf_op jit(solution)/shard_map/psum | solution.py:209
  425.2 1.1 convert_reduce_fusion.1
  426.5 1.3 fusion.25
  427.8 1.3 convolution_bitcast_fusion
  429.1 21.4 %all_gather.19 = bf16[1024,1,2,96]{0,3,2,1:T(8,128)(2,1)S(1)} all-gather(bf16[128,1,2,96]{0,3,2,1:T(8,128)(2,1)S(1)} %fusion.25), channel_id=1, replica_groups=mesh['row'=8,'col'=8,'smp'=8] {'row'}, dimensions={0}, use_global_device_ids=true | all-gather | bytes 442368 | tf_op jit(solution)/shard_map/all_gather | solution.py:196
  450.6 0.5 fusion.153
  451.1 0.3 fusion.44
  451.4 0.4 fusion.30
  451.8 0.9 fusion.17
  452.8 79.6 %all-reduce.11.cloned.1.call-done = bf16[1,128,768]{2,1,0:T(8,128)(2,1)} async-done(((bf16[1,128,768]{2,1,0:T(8,128)(2,1)}), bf16[1,128,768]{2,1,0:T(8,128)(2,1)}) %all-reduce.11.cloned.1.call-update) | async-done | bytes 196624 | tf_op jit(solution)/shard_map/psum | solution.py:209
  532.4 1.1 convert_reduce_fusion.5
  533.7 0.2 fusion.35
  533.9 0.6 copy.49
  (88 shorter events, 2.4 us)
Async XLA Ops:
  7.2 11.7 %copy-start = (bf16[128,4,16]{0,2,1:T(8,128)(2,1)S(1)}, bf16[128,4,16]{0,2,1:T(8,128)(2,1)}, u32[]{:S(2)}) copy-start(bf16[128,4,16]{0,2,1:T(8,128)(2,1)} %param.25) | copy-start | bytes 49156
  7.2 12.0 %copy-start.8 = (f32[1,3]{1,0:T(1,128)S(1)}, f32[1,3]{1,0:T(1,128)}, u32[]{:S(2)}) copy-start(f32[1,3]{1,0:T(1,128)} %param.21) | copy-start | bytes 40
  8.5 11.6 %all-to-all-start.1 = ((s32[8,1,128]{2,1,0:T(1,128)}), s32[8,1,128]{2,1,0:T(1,128)S(1)}, u32[]{:S(2)}, u32[]{:S(2)}) async-start(s32[8,1,128]{2,1,0:T(1,128)} %stack.75), calls=%async_computation.1 | async-start | bytes 8192 | tf_op jit(solution)/shard_map/all_to_all | solution.py:152
  21.9 21.4 %copy-start.6 = (f32[3,8192]{1,0:T(4,128)S(1)}, f32[3,8192]{1,0:T(4,128)}, u32[]{:S(2)}) copy-start(f32[3,8192]{1,0:T(4,128)} %param.17) | copy-start | bytes 294916
  21.9 94.7 %all-to-all-start = ((bf16[4,128,128,1,16]{2,4,3,0,1:T(8,128)(2,1)}), bf16[4,128,128,1,16]{2,4,3,0,1:T(8,128)(2,1)S(1)}, u32[]{:S(2)}, u32[]{:S(2)}) async-start(bf16[4,128,128,1,16]{2,4,3,0,1:T(8,128)(2,1)} %bitcast.261), calls=%async_computation | async-start | bytes 4194304 | tf_op jit(solution)/shard_map/all_to_all | solution.py:74
  38.3 11.0 %copy-start.7 = (f32[4,768]{1,0:T(4,128)S(1)}, f32[4,768]{1,0:T(4,128)}, u32[]{:S(2)}) copy-start(f32[4,768]{1,0:T(4,128)} %param.24) | copy-start | bytes 36868
  38.3 11.0 %copy-start.14 = (s32[128]{0:T(128)S(1)}, s32[128]{0:T(128)}, u32[]{:S(2)}) copy-start(s32[128]{0:T(128)} %param.18) | copy-start | bytes 1540
  38.3 171.7 %all-reduce.5.cloned.1.call-start = ((), (), s32[]{:S(2)}) async-start(), calls=%async_computation.2 | async-start | bytes 393216 | tf_op jit(solution)/shard_map/psum | solution.py:209
  43.4 6.2 %copy-start.11 = (f32[1,3,128]{2,0,1:T(1,128)S(1)}, f32[1,3,128]{2,0,1:T(1,128)}, u32[]{:S(2)}) copy-start(f32[1,3,128]{2,0,1:T(1,128)} %param.23) | copy-start | bytes 4612
  43.4 6.3 %copy-start.5 = (bf16[128,768]{1,0:T(8,128)(2,1)S(1)}, bf16[128,768]{1,0:T(8,128)(2,1)}, u32[]{:S(2)}) copy-start(bf16[128,768]{1,0:T(8,128)(2,1)} %param.15) | copy-start | bytes 589828
  43.4 8.1 %copy-start.12 = (s32[128]{0:T(128)S(1)}, s32[128]{0:T(128)}, u32[]{:S(2)}) copy-start(s32[128]{0:T(128)} %param.20) | copy-start | bytes 1540
  43.4 50.2 %copy-start.10 = (f32[4,16]{1,0:T(4,128)S(1)}, f32[4,16]{1,0:T(4,128)}, u32[]{:S(2)}) copy-start(f32[4,16]{1,0:T(4,128)} %param.26) | copy-start | bytes 772
  46.0 70.5 %copy-start.9 = (s32[128]{0:T(128)S(1)}, s32[128]{0:T(128)}, u32[]{:S(2)}) copy-start(s32[128]{0:T(128)} %param.19) | copy-start | bytes 1540
  124.6 193.5 %all-reduce.7.cloned.1.call-start = ((), (), s32[]{:S(2)}) async-start(), calls=%async_computation.3 | async-start | bytes 393216 | tf_op jit(solution)/shard_map/psum | solution.py:209
  127.3 108.0 %copy-start.1 = (f32[2,128,1024]{2,1,0:T(8,128)S(1)}, f32[2,128,1024]{2,1,0:T(8,128)}, u32[]{:S(2)}) copy-start(f32[2,128,1024]{2,1,0:T(8,128)} %copy.44) | copy-start | bytes 3145732
  238.4 186.8 %all-reduce.9.cloned.1.call-start = ((), (), s32[]{:S(2)}) async-start(), calls=%async_computation.4 | async-start | bytes 393216 | tf_op jit(solution)/shard_map/psum | solution.py:209
  241.2 102.3 %copy-start.2 = (f32[2,128,1024]{2,1,0:T(8,128)S(1)}, f32[2,128,1024]{2,1,0:T(8,128)}, u32[]{:S(2)}) copy-start(f32[2,128,1024]{2,1,0:T(8,128)} %copy.46) | copy-start | bytes 3145732
  343.5 1.2 copy-start.4
  345.7 186.8 %all-reduce.11.cloned.1.call-start = ((), (), s32[]{:S(2)}) async-start(), calls=%async_computation.5 | async-start | bytes 393216 | tf_op jit(solution)/shard_map/psum | solution.py:209
  451.1 82.6 %copy-start.13 = (bf16[3,768]{1,0:T(4,128)(2,1)S(1)}, bf16[3,768]{1,0:T(4,128)(2,1)}, u32[]{:S(2)}) copy-start(bf16[3,768]{1,0:T(4,128)(2,1)} %param.29) | copy-start | bytes 13828
  533.5 1.1 copy-start.3
Sparse Core Ops, SparseCore 0:
  124.7 85.1 all-reduce.4
  238.5 79.5 all-reduce.6
  345.8 79.4 all-reduce.8
  452.9 79.5 all-reduce.10
